TPU v7x, 256 devices: a whole 4x4x8 slice. The times are simulated.
256 devices in a mesh: grp: 32 (over y, z_lo, core), tp: 8 (over x, z_hi).
Axes of the slice: x: 4, y: 4, z: 8 (z_hi: 2, z_lo: 4; z = z_hi * 4 + z_lo), core: 2. Of those that a mesh axis runs over, the one named last changes fastest.
Arguments:
- tok_ids: int32 [8192], P('grp'), may hold values from 0 to 16383
- accept: int32 [8192], P('grp'), may hold values 0 or 1
- sub_ids: int32 [8192], P('grp'), may hold values from 0 to 16383
- cache_len: int32 [32], replicated, may hold values from 256 to 3840, as said below
- spill: int32 [32], replicated, may hold values from 0 to 1792, as said below
- embed: bfloat16 [16384, 2048], P('grp', 'tp'), may hold values from -6 to 6
- attn_gain: float32 [2048], replicated, may hold values from 0.25 to 1.75
- w_query: bfloat16 [2048, 2048], P(None, 'tp'), may hold values from -0.125 to 0.125
- w_key: bfloat16 [2048, 512], P(None, 'tp'), as said below
- w_value: bfloat16 [2048, 512], P(None, 'tp'), as said below
- w_out: bfloat16 [2048, 2048], P('tp'), may hold values from -2.5 to 2.5
- mlp_gain: float32 [2048], replicated, may hold values from 0.25 to 1.75
- w_gate: bfloat16 [2048, 5632], P(None, 'tp'), may hold values from -0.125 to 0.125
- w_up: bfloat16 [2048, 5632], P(None, 'tp'), may hold values from -0.125 to 0.125
- w_down: bfloat16 [5632, 2048], P('tp'), may hold values from -0.078125 to 0.078125
- cache_keys: bfloat16 [65536, 512], P('grp', 'tp'), may hold values from -320 to 320, as said below
- cache_values: bfloat16 [65536, 512], P('grp', 'tp'), may hold values from -8 to 8, as said below
Outputs:
- first_out: bfloat16 [8192, 2048], P('grp', 'tp')
- second_out: bfloat16 [8192, 2048], P('grp', 'tp')
Inputs may be any that keep to these rules, and one draw needn't show every extreme that they name: Request g keeps cache_len[g] - spill[g] >= 256 positions in slots from 0 of store g and spill[g] positions in the last slots of store (g xor 1); for every g, cache_len[g] - spill[g] + spill[g xor 1] <= 2048. Of each pair of groups 2k, 2k + 1 at most one has spill above 0. `w_key`: the 2 stored copies of a key-value head are equal. `w_value`: the 2 stored copies of a key-value head are equal. `cache_keys`: the 2 stored copies of a key-value head are equal. `cache_values`: the 2 stored copies of a key-value head are equal.
All inputs are finite; a program needn't handle non-finite values. No bound on the sum of `accept` on one device may be relied on, other than what follows from the above.
Results may differ from a plain program's by a relative error of at most 0.024.
Values may be sent and summed in bfloat16 or wider, within the bound.
No kernel may reach another device: no remote copies, remote signals or barrier semaphores. Data moves between devices by JAX's collectives and lax.ppermute only.
A program may use at most 128 MiB of HBM per device.

v0:
```python
import jax
import jax.numpy as jnp
from jax import lax
from jax.sharding import PartitionSpec as P

HD = 64
EPSILON = 1e-05
SENTINEL = -1e30


def swapped(array, axis, bit):
    return lax.ppermute(array, axis, [(i, i ^ 1 << bit) for i in range(lax.axis_size(axis))])


def rms_normed(values, gain):
    square = jnp.mean(values * values, axis=-1, keepdims=True)
    return (values * lax.rsqrt(square + EPSILON) * gain).astype(jnp.bfloat16)


def rotate(vectors, positions):
    half = vectors.shape[-1] // 2
    exponent = jnp.arange(half, dtype=jnp.float32) * (-2.0 / vectors.shape[-1])
    freqs = jnp.power(jnp.float32(10000.0), exponent)
    angles = positions.astype(jnp.float32)[:, None] * freqs[None, :]
    cosine = jnp.cos(angles)[:, None, :]
    sine = jnp.sin(angles)[:, None, :]
    first = vectors[..., :half]
    second = vectors[..., half:]
    return jnp.concatenate(
        [first * cosine - second * sine, second * cosine + first * sine], axis=-1
    )


def partial_attention(query, keys, values, valid):
    scores = jnp.einsum("bcgd,kcd->bcgk", query, keys, preferred_element_type=jnp.float32) * 0.125
    scores = jnp.where(valid, scores, SENTINEL)
    top = jnp.max(scores, axis=-1)
    weights = jnp.where(valid, jnp.exp(scores - top[..., None]), 0.0)
    total = jnp.sum(weights, axis=-1)
    weighted = jnp.einsum(
        "bcgk,kcd->bcgd", weights.astype(jnp.bfloat16), values, preferred_element_type=jnp.float32
    )
    return (weighted, top, total)


def on_device(
    tok_ids,
    accept,
    sub_ids,
    cache_len,
    spill,
    embed,
    attn_gain,
    w_query,
    w_key,
    w_value,
    w_out,
    mlp_gain,
    w_gate,
    w_up,
    w_down,
    cache_keys,
    cache_values,
):
    block = tok_ids.shape[0]
    slots = cache_keys.shape[0]
    local_vocab = embed.shape[0]
    query_local = w_query.shape[1] // HD
    stored_local = w_key.shape[1] // HD
    per_stored = query_local // stored_local
    group_index = lax.axis_index("grp")
    shard_index = lax.axis_index("tp")
    own_count = cache_len[group_index] - spill[group_index]
    far_count = spill[group_index]
    positions = cache_len[group_index] + jnp.arange(block, dtype=jnp.int32)
    slot_ids = jnp.arange(slots, dtype=jnp.int32)
    tail_ids = slot_ids[block:]
    store_keys = cache_keys.reshape(slots, stored_local, HD)
    store_values = cache_values.reshape(slots, stored_local, HD)
    block_valid = jnp.ones((block,), dtype=bool)
    second_ids = jnp.where(accept == 1, sub_ids, tok_ids)
    vocab_base = group_index * local_vocab
    vocab_ids = jnp.arange(local_vocab, dtype=jnp.int32)

    def lookup(id_list):
        onehot = (id_list[:, None] - vocab_base == vocab_ids[None, :]).astype(jnp.bfloat16)
        return jnp.dot(onehot, embed, preferred_element_type=jnp.float32)

    all_first, all_second = (
        lax.all_gather(tok_ids, "grp", axis=0, tiled=True),
        lax.all_gather(second_ids, "grp", axis=0, tiled=True),
    )
    first_rows = lax.psum_scatter(
        lookup(all_first).astype(jnp.bfloat16), "grp", scatter_dimension=0, tiled=True
    )
    second_rows = lax.psum_scatter(
        lookup(all_second).astype(jnp.bfloat16), "grp", scatter_dimension=0, tiled=True
    )
    tail_keys, tail_values = swapped((cache_keys[block:], cache_values[block:]), "grp", 0)
    far_keys = tail_keys.reshape(slots - block, stored_local, HD)
    far_values = tail_values.reshape(slots - block, stored_local, HD)
    far_valid = tail_ids >= slots - far_count

    def denoise(x_part):
        width = x_part.shape[1]
        x_full = lax.all_gather(x_part, "tp", axis=1, tiled=True)
        normed = rms_normed(x_full.astype(jnp.float32), attn_gain)
        query = rotate(
            jnp.dot(normed, w_query, preferred_element_type=jnp.float32).reshape(
                block, query_local, HD
            ),
            positions,
        )
        query = query.astype(jnp.bfloat16).reshape(block, stored_local, per_stored, HD)
        new_keys = rotate(
            jnp.dot(normed, w_key, preferred_element_type=jnp.float32).reshape(
                block, stored_local, HD
            ),
            positions,
        ).astype(jnp.bfloat16)
        new_values = (
            jnp.dot(normed, w_value, preferred_element_type=jnp.float32)
            .reshape(block, stored_local, HD)
            .astype(jnp.bfloat16)
        )
        own_valid = slot_ids < own_count
        keys = jnp.concatenate([store_keys, far_keys, new_keys], axis=0)
        values = jnp.concatenate([store_values, far_values, new_values], axis=0)
        valid = jnp.concatenate([own_valid, far_valid, block_valid])
        weighted, top, total = partial_attention(query, keys, values, valid)
        attended = weighted / total[..., None]
        mixed = attended.reshape(block, query_local * HD).astype(jnp.bfloat16)
        head_term = jnp.dot(mixed, w_out, preferred_element_type=jnp.float32)
        head_sum = lax.psum(head_term.astype(jnp.bfloat16), "tp").astype(jnp.float32)
        resid_full = (x_full.astype(jnp.float32) + head_sum).astype(jnp.bfloat16)
        resid_part = lax.dynamic_slice_in_dim(resid_full, shard_index * width, width, 1)
        normed_mlp = rms_normed(resid_full.astype(jnp.float32), mlp_gain)
        gate = jnp.dot(normed_mlp, w_gate, preferred_element_type=jnp.float32)
        lift = jnp.dot(normed_mlp, w_up, preferred_element_type=jnp.float32)
        hidden = (jax.nn.silu(gate) * lift).astype(jnp.bfloat16)
        down_term = jnp.dot(hidden, w_down, preferred_element_type=jnp.float32)
        down_part = lax.psum_scatter(
            down_term.astype(jnp.bfloat16), "tp", scatter_dimension=1, tiled=True
        ).astype(jnp.float32)
        return (resid_part.astype(jnp.float32) + down_part).astype(jnp.bfloat16)

    return (denoise(first_rows), denoise(second_rows))


def solution(mesh):
    placed = (
        P("grp"),
        P("grp"),
        P("grp"),
        P(),
        P(),
        P("grp", "tp"),
        P(),
        P(None, "tp"),
        P(None, "tp"),
        P(None, "tp"),
        P("tp", None),
        P(),
        P(None, "tp"),
        P(None, "tp"),
        P("tp", None),
        P("grp", "tp"),
        P("grp", "tp"),
    )
    return jax.shard_map(
        on_device,
        mesh=mesh,
        in_specs=placed,
        out_specs=(P("grp", "tp"), P("grp", "tp")),
        check_vma=False,
    )
```

profile of v0, /device:TPU:8, one launch (start us, length us, event | category | flops | bytes accessed | tf_op | source)
XLA Modules:
  0.0 960.8 jit_solution(10995285730689573226)
XLA Ops:
  7.2 0.9 compare_select_fusion
  8.1 37.6 %all-gather.1 = s32[32,1,256]{2,1,0:T(1,128)S(1)} all-gather(s32[1,1,256]{2,1,0:T(1,128)S(1)} %bitcast.193), channel_id=1, replica_groups=mesh['grp'=32,'tp'=8] {'grp'}, dimensions={0}, use_global_device_ids=true | all-gather | bytes 33792 | tf_op jit(solution)/shard_map/all_gather | solution.py:91
  45.7 38.2 %all-gather = s32[32,1,256]{2,1,0:T(1,128)S(1)} all-gather(s32[1,1,256]{2,1,0:T(1,128)} %bitcast.192), channel_id=1, replica_groups=mesh['grp'=32,'tp'=8] {'grp'}, dimensions={0}, use_global_device_ids=true | all-gather | bytes 33792 | tf_op jit(solution)/shard_map/all_gather | solution.py:90
  83.9 6.3 fusion.10
  90.2 0.9 copy-done.11
  91.1 5.4 fusion.11
  96.6 131.9 %reduce-scatter.9.cloned.1.call-done = bf16[256,256]{1,0:T(8,128)(2,1)} async-done(((bf16[8192,256]{1,0:T(8,128)(2,1)}), bf16[256,256]{1,0:T(8,128)(2,1)}) %reduce-scatter.9.cloned.1.call-update) | async-done | bytes 131088 | tf_op jit(solution)/shard_map/reduce_scatter | solution.py:96
  228.6 151.1 %reduce-scatter.5.cloned.1.call-done = bf16[256,256]{1,0:T(8,128)(2,1)} async-done(((bf16[8192,256]{1,0:T(8,128)(2,1)}), bf16[256,256]{1,0:T(8,128)(2,1)}) %reduce-scatter.5.cloned.1.call-update) | async-done | bytes 131088 | tf_op jit(solution)/shard_map/reduce_scatter | solution.py:93
  379.8 0.7 slice.35
  380.5 1.6 slice.33
  382.1 0.5 collective-permute-start
  382.6 0.6 dynamic_slice.14
  383.2 0.6 dynamic_slice.15
  385.7 0.7 add_convert_fusion.4
  386.5 0.2 multiply_cosine_fusion
  386.7 73.9 %all-gather.7.cloned.1.call-done = bf16[256,2048]{1,0:T(8,128)(2,1)} async-done(((bf16[256,256]{1,0:T(8,128)(2,1)}), bf16[256,2048]{1,0:T(8,128)(2,1)}) %all-gather.7.cloned.1.call-update) | async-done | bytes 1048592 | tf_op jit(solution)/shard_map/all_gather | solution.py:106
  460.6 1.5 fusion.34
  462.1 58.2 %all-gather.5.cloned.1.call-done = bf16[256,2048]{1,0:T(8,128)(2,1)} async-done(((bf16[256,256]{1,0:T(8,128)(2,1)}), bf16[256,2048]{1,0:T(8,128)(2,1)}) %all-gather.5.cloned.1.call-update) | async-done | bytes 1048592 | tf_op jit(solution)/shard_map/all_gather | solution.py:106
  520.3 1.7 fusion.30
  522.0 2.3 fusion.114
  524.3 0.7 fusion.118
  525.0 0.1 subtract_convert_fusion
  525.1 0.5 convolution_bitcast_fusion
  525.6 0.5 convolution_bitcast_fusion.1
  526.1 0.2 fusion.99
  526.3 8.1 fusion.61
  534.5 14.5 %bitcast_reduce_fusion = (f32[256,4]{0,1:T(4,128)S(1)}, f32[256,4]{0,1:T(4,128)S(1)}, f32[4096,256,4]{1,0,2:T(8,128)}) fusion(pred[4096]{0:T(1024)(128)(4,1)S(1)} %pad_add_fusion, f32[4096,256,4]{1,0,2:T(8,128)} %fusion.61, bf16[256,4,32]{0,2,1:T(8,128)(2,1)S(1)} %get-tuple-element.13, bf16[256,4,32]{0,2,1:T(8,128)(2,1)S(1)} %get-tuple-element.12, ...), kind=kOutput, calls=%fused_computation.1 | convolution fusion | flops 564393984 | bytes 34222080 | tf_op jit(solution)/shard_map/bcgd,kcd->bcgk/dot_general | solution.py:35
  549.0 14.2 %fusion.8 = (f32[256,4]{0,1:T(4,128)S(1)}, f32[256,4]{0,1:T(4,128)S(1)}) fusion(f32[4096,256,4]{1,0,2:T(8,128)} %get-tuple-element.26, f32[256,4]{0,1:T(4,128)S(1)} %get-tuple-element.4, pred[4096]{0:T(1024)(128)(4,1)S(1)} %pad_add_fusion, f32[256,4]{0,1:T(4,128)S(1)} %get-tuple-element.5, f32[4096,256,4]{1,0,2:T(8,128)} %fusion.61), kind=kLoop, calls=%fused_computation.16 | loop fusion | flops 41940992 | bytes 33574912 | tf_op jit(solution)/shard_map/reduce_sum | solution.py:39
  563.2 0.5 fusion.46
  563.8 5.4 fusion.51
  569.3 1.5 convolution_convert_fusion.3
  570.8 0.5 fusion.47
  571.3 5.1 fusion.57
  576.4 1.5 convolution_convert_fusion.1
  577.9 0.3 reduce-scatter.7.cloned.1.call-start
  578.2 190.4 %all-reduce.3.cloned.1.call-done = (bf16[256,2048]{1,0:T(8,128)(2,1)}, bf16[256,2048]{1,0:T(8,128)(2,1)}) async-done(((bf16[256,2048]{1,0:T(8,128)(2,1)}, bf16[256,2048]{1,0:T(8,128)(2,1)}), (bf16[256,2048]{1,0:T(8,128)(2,1)}, bf16[256,2048]{1,0:T(8,128)(2,1)})) %all-reduce.3.cloned.1.call-update) | async-done | bytes 2097168 | tf_op jit(solution)/shard_map/psum | solution.py:134
  768.6 2.2 fusion.24
  770.8 1.0 copy-done.4
  771.8 1.9 fusion.78
  773.8 6.6 convolution_convert_fusion.2
  780.5 2.2 fusion.27
  782.7 0.9 copy-done.5
  783.7 1.9 fusion.74
  785.6 6.6 convolution_convert_fusion
  792.3 72.7 %reduce-scatter.7.cloned.1.call-done = bf16[256,256]{1,0:T(8,128)(2,1)} async-done(((bf16[256,2048]{1,0:T(8,128)(2,1)}), bf16[256,256]{1,0:T(8,128)(2,1)}) %reduce-scatter.7.cloned.1.call-update) | async-done | bytes 131088 | tf_op jit(solution)/shard_map/reduce_scatter | solution.py:142
  865.0 1.7 add_convert_fusion.1
  866.6 85.6 %reduce-scatter.11.cloned.1.call-done = bf16[256,256]{1,0:T(8,128)(2,1)} async-done(((bf16[256,2048]{1,0:T(8,128)(2,1)}), bf16[256,256]{1,0:T(8,128)(2,1)}) %reduce-scatter.11.cloned.1.call-update) | async-done | bytes 131088 | tf_op jit(solution)/shard_map/reduce_scatter | solution.py:142
  952.3 1.7 add_convert_fusion
  (77 shorter events, 0.6 us)
Async XLA Ops:
  7.2 766.6 %copy-start = (bf16[704,2048]{1,0:T(8,128)(2,1)S(1)}, bf16[704,2048]{1,0:T(8,128)(2,1)}, u32[]{:S(2)}) copy-start(bf16[704,2048]{1,0:T(8,128)(2,1)} %param.31) | copy-start | bytes 8650756
  7.2 221.3 %reduce-scatter.9.cloned.1.call-start = ((), (), s32[]{:S(2)}) async-start(), calls=%async_computation.7 | async-start | bytes 4325376 | tf_op jit(solution)/shard_map/reduce_scatter | solution.py:96
  90.1 0.9 copy-start.11
  90.2 289.5 %reduce-scatter.5.cloned.1.call-start = ((), (), s32[]{:S(2)}) async-start(), calls=%async_computation.4 | async-start | bytes 4325376 | tf_op jit(solution)/shard_map/reduce_scatter | solution.py:93
  96.5 283.2 %copy-start.6 = (bf16[2048,64]{0,1:T(8,128)(2,1)S(1)}, bf16[2048,64]{0,1:T(8,128)(2,1)}, u32[]{:S(2)}) copy-start(bf16[2048,64]{0,1:T(8,128)(2,1)} %param.32) | copy-start | bytes 786436
  96.5 286.1 %copy-start.16 = (s32[32]{0:T(128)S(1)}, s32[32]{0:T(128)}, u32[]{:S(2)}) copy-start(s32[32]{0:T(128)} %param.20) | copy-start | bytes 388
  96.5 286.7 %copy-start.17 = (s32[32]{0:T(128)S(1)}, s32[32]{0:T(128)}, u32[]{:S(2)}) copy-start(s32[32]{0:T(128)} %param.21) | copy-start | bytes 388
  96.5 425.4 %copy-start.14 = (f32[2048]{0:T(1024)S(1)}, f32[2048]{0:T(1024)}, u32[]{:S(2)}) copy-start(f32[2048]{0:T(1024)} %param.23) | copy-start | bytes 24580
  96.6 364.0 %all-gather.7.cloned.1.call-start = ((), (), s32[]{:S(2)}) async-start(), calls=%async_computation.8 | async-start | bytes 1179648 | tf_op jit(solution)/shard_map/all_gather | solution.py:106
  228.5 291.7 %all-gather.5.cloned.1.call-start = ((), (), s32[]{:S(2)}) async-start(), calls=%async_computation.5 | async-start | bytes 1179648 | tf_op jit(solution)/shard_map/all_gather | solution.py:106
  379.7 388.9 %all-reduce.3.cloned.1.call-start = ((), (), s32[]{:S(2)}) async-start(), calls=%async_computation.10 | async-start | bytes 4194304 | tf_op jit(solution)/shard_map/psum | solution.py:134
  380.5 145.9 %collective-permute-start.1 = (bf16[1792,64]{0,1:T(8,128)(2,1)}, bf16[1792,64]{0,1:T(8,128)(2,1)S(1)}, u32[]{:S(2)}, u32[]{:S(2)}) collective-permute-start(bf16[1792,64]{0,1:T(8,128)(2,1)} %slice.35), channel_id=1, source_target_pairs={{0,8},{8,0},{16,24},{24,16},{32,40},{40,32},{48,56},{56,48},{64,72... | collective-permute-start | bytes 688136 | tf_op jit(solution)/shard_map/ppermute | solution.py:12
  382.1 181.6 %collective-permute-start = (bf16[1792,64]{0,1:T(8,128)(2,1)}, bf16[1792,64]{0,1:T(8,128)(2,1)}, u32[]{:S(2)}, u32[]{:S(2)}) collective-permute-start(bf16[1792,64]{0,1:T(8,128)(2,1)} %slice.33), channel_id=1, source_target_pairs={{0,8},{8,0},{16,24},{24,16},{32,40},{40,32},{48,56},{56,48},{64,72... | collective-permute-start | bytes 688136 | tf_op jit(solution)/shard_map/ppermute | solution.py:12
  520.3 4.0 copy-start.3
  520.3 4.0 copy-start.10
  521.9 3.1 copy-start.2
  521.9 3.1 copy-start.12
  534.5 29.3 %slice-start = ((s8[16777216]{0:T(1024)(128)(4,1)}), s8[4194304]{0:T(1024)(128)(4,1)S(1)}, s32[]{:S(2)}) async-start(s8[16777216]{0:T(1024)(128)(4,1)} %bitcast.174), calls=%async_computation.11 | async-start | bytes 8388608
  534.5 29.3 %slice-start.1 = ((s8[16777216]{0:T(1024)(128)(4,1)}), s8[4194304]{0:T(1024)(128)(4,1)S(1)}, s32[]{:S(2)}) async-start(s8[16777216]{0:T(1024)(128)(4,1)} %bitcast.174), calls=%async_computation.12 | async-start | bytes 8388608
  534.5 29.3 %slice-start.2 = ((s8[16777216]{0:T(1024)(128)(4,1)}), s8[4194304]{0:T(1024)(128)(4,1)S(1)}, s32[]{:S(2)}) async-start(s8[16777216]{0:T(1024)(128)(4,1)} %bitcast.174), calls=%async_computation.13 | async-start | bytes 8388608
  549.0 14.2 %copy-start.13 = (bf16[2048,64]{0,1:T(8,128)(2,1)S(1)}, bf16[2048,64]{0,1:T(8,128)(2,1)}, u32[]{:S(2)}) copy-start(bf16[2048,64]{0,1:T(8,128)(2,1)} %param.26) | copy-start | bytes 786436
  549.0 14.8 %slice-start.3 = ((s8[16777216]{0:T(1024)(128)(4,1)}), s8[4194304]{0:T(1024)(128)(4,1)S(1)}, s32[]{:S(2)}) async-start(s8[16777216]{0:T(1024)(128)(4,1)} %bitcast.174), calls=%async_computation.14 | async-start | bytes 8388608
  549.0 14.8 %copy-start.7 = (bf16[2048,64]{0,1:T(8,128)(2,1)S(1)}, bf16[2048,64]{0,1:T(8,128)(2,1)}, u32[]{:S(2)}) copy-start(bf16[2048,64]{0,1:T(8,128)(2,1)} %param.33) | copy-start | bytes 786436
  563.2 8.1 slice-start.4
  563.8 5.5 copy-start.1
  563.8 7.5 slice-start.5
  563.8 7.5 slice-start.6
  563.8 7.5 slice-start.7
  577.9 194.0 %copy-start.15 = (f32[2048]{0:T(1024)S(1)}, f32[2048]{0:T(1024)}, u32[]{:S(2)}) copy-start(f32[2048]{0:T(1024)} %param.28) | copy-start | bytes 24580
  577.9 287.1 %reduce-scatter.7.cloned.1.call-start = ((), (), s32[]{:S(2)}) async-start(), calls=%async_computation.6 | async-start | bytes 1179648 | tf_op jit(solution)/shard_map/reduce_scatter | solution.py:142
  768.6 3.2 copy-start.8
  770.8 1.0 copy-start.4
  780.5 171.8 %reduce-scatter.11.cloned.1.call-start = ((), (), s32[]{:S(2)}) async-start(), calls=%async_computation.9 | async-start | bytes 1179648 | tf_op jit(solution)/shard_map/reduce_scatter | solution.py:142
  780.5 3.2 copy-start.9
  782.7 1.0 copy-start.5
Sparse Core Ops, SparseCore 0:
  90.3 138.1 reduce-scatter.8
  231.0 148.6 reduce-scatter.4
  382.2 78.3 all-gather.6
  462.9 57.3 all-gather.4
  578.0 190.5 all-reduce.2
  780.6 84.3 reduce-scatter.6
  869.4 82.7 reduce-scatter.10
where the time goes:
time: 961 us
  waiting for transfers between devices  764 us (80%)
  blocking collectives  75.8 us (8%)
  matrix products  70 us (7%)
  other arithmetic  27.1 us (3%)
  between operations  16.5 us (2%)
    psum x1, waiting for transfers between devices, denoise(): lax.psum(head_term.astype(jnp.bfloat16), 'tp').astype(jnp.float32)  190 us
    reduce_scatter x2, waiting for transfers between devices, denoise(): lax.psum_scatter(down_term.astype(jnp.bfloat16), 'tp', scatter_dimension=...  158 us
    reduce_scatter x1, waiting for transfers between devices, on_device(): lax.psum_scatter(lookup(all_first).astype(jnp.bfloat16), 'grp', scatter_d...  151 us
    all_gather x2, waiting for transfers between devices, denoise(): x_full = lax.all_gather(x_part, 'tp', axis=1, tiled=True)  132 us
    reduce_scatter x1, waiting for transfers between devices, on_device(): lax.psum_scatter(lookup(all_second).astype(jnp.bfloat16), 'grp', scatter_...  132 us
    all_gather x1, blocking collectives, on_device(): lax.all_gather(tok_ids, 'grp', axis=0, tiled=True)  38.2 us
    all_gather x1, blocking collectives, on_device(): lax.all_gather(second_ids, 'grp', axis=0, tiled=True)  37.6 us
    dot_general x2, matrix products, partial_attention(): jnp.einsum('bcgd,kcd->bcgk', query, keys, preferred_element_type=jnp.floa...  22.6 us
  transfers between devices with their start and end apart: 9, of which 7 were waited for; matrix products, arithmetic and copies ran while one was open for 7% of the time, Pallas kernels for 0%

commit v1 on v0

--- a/solution.py
+++ b/solution.py
@@ -87,7 +87,9 @@
         return jnp.dot(onehot, embed, preferred_element_type=jnp.float32)
 
     all_first, all_second = (
-        lax.all_gather(tok_ids, "grp", axis=0, tiled=True),
+        jnp.concatenate(
+            lax.all_to_all(jnp.stack([tok_ids] * lax.axis_size("grp")), "grp", 0, 0), axis=0
+        ),
         lax.all_gather(second_ids, "grp", axis=0, tiled=True),
     )
     first_rows = lax.psum_scatter(

time: 961 us -> 932 us (0.970)
  blocking collectives: 75.8 us -> 36.1 us
    all_gather x1 -> x0, blocking collectives: 38.2 us -> none  [on_device(): lax.all_gather(tok_ids, 'grp', axis=0, tiled=True)]
  transfers between devices with their start and end apart: 9 -> 10, of which waited for: 7 -> 7; matrix products, arithmetic and copies ran while one was open for 7% -> 7% of each run, Pallas kernels for 0% -> 0%
where the time goes in v1:
time: 932 us; the launch traced here: 931 us
  waiting for transfers between devices  764 us (82%)
  matrix products  70 us (8%)
  blocking collectives  36.1 us (4%)
  other arithmetic  27 us (3%)
  between operations  16.5 us (2%)
  starting transfers between devices  10.2 us (1%)
    psum x1, waiting for transfers between devices, denoise(): lax.psum(head_term.astype(jnp.bfloat16), 'tp').astype(jnp.float32)  190 us
    reduce_scatter x2, waiting for transfers between devices, denoise(): lax.psum_scatter(down_term.astype(jnp.bfloat16), 'tp', scatter_dimension=...  158 us
    reduce_scatter x1, waiting for transfers between devices, on_device(): lax.psum_scatter(lookup(all_first).astype(jnp.bfloat16), 'grp', scatter_d...  152 us
    all_gather x2, waiting for transfers between devices, denoise(): x_full = lax.all_gather(x_part, 'tp', axis=1, tiled=True)  131 us
    reduce_scatter x1, waiting for transfers between devices, on_device(): lax.psum_scatter(lookup(all_second).astype(jnp.bfloat16), 'grp', scatter_...  131 us
    all_gather x1, blocking collectives, on_device(): lax.all_gather(second_ids, 'grp', axis=0, tiled=True)  36.1 us
    dot_general x2, matrix products, partial_attention(): jnp.einsum('bcgd,kcd->bcgk', query, keys, preferred_element_type=jnp.floa...  22.7 us
  transfers between devices with their start and end apart: 10, of which 7 were waited for; matrix products, arithmetic and copies ran while one was open for 7% of the time, Pallas kernels for 0%

profile of v1, /device:TPU:8, one launch (start us, length us, event | category | flops | bytes accessed | tf_op | source)
XLA Modules:
  0.0 931.3 jit_solution(10961414832630257322)
XLA Ops:
  7.2 1.5 stack.2
  8.6 9.1 all-to-all-start
  17.8 0.7 compare_select_fusion
  18.6 36.1 %all-gather = s32[32,1,256]{2,1,0:T(1,128)S(1)} all-gather(s32[1,1,256]{2,1,0:T(1,128)S(1)} %bitcast.191), channel_id=1, replica_groups=mesh['grp'=32,'tp'=8] {'grp'}, dimensions={0}, use_global_device_ids=true | all-gather | bytes 33792 | tf_op jit(solution)/shard_map/all_gather | solution.py:93
  54.7 6.3 fusion.10
  61.1 0.9 copy-done.11
  61.9 5.4 fusion.11
  67.5 131.0 %reduce-scatter.9.cloned.1.call-done = bf16[256,256]{1,0:T(8,128)(2,1)} async-done(((bf16[8192,256]{1,0:T(8,128)(2,1)}), bf16[256,256]{1,0:T(8,128)(2,1)}) %reduce-scatter.9.cloned.1.call-update) | async-done | bytes 131088 | tf_op jit(solution)/shard_map/reduce_scatter | solution.py:98
  198.6 152.3 %reduce-scatter.5.cloned.1.call-done = bf16[256,256]{1,0:T(8,128)(2,1)} async-done(((bf16[8192,256]{1,0:T(8,128)(2,1)}), bf16[256,256]{1,0:T(8,128)(2,1)}) %reduce-scatter.5.cloned.1.call-update) | async-done | bytes 131088 | tf_op jit(solution)/shard_map/reduce_scatter | solution.py:95
  350.9 0.7 slice.35
  351.7 1.6 slice.33
  353.3 0.5 collective-permute-start
  353.8 0.6 dynamic_slice.14
  354.4 0.6 dynamic_slice.15
  356.9 0.7 add_convert_fusion.4
  357.6 0.2 multiply_cosine_fusion
  357.8 73.1 %all-gather.6.cloned.1.call-done = bf16[256,2048]{1,0:T(8,128)(2,1)} async-done(((bf16[256,256]{1,0:T(8,128)(2,1)}), bf16[256,2048]{1,0:T(8,128)(2,1)}) %all-gather.6.cloned.1.call-update) | async-done | bytes 1048592 | tf_op jit(solution)/shard_map/all_gather | solution.py:108
  430.9 1.5 fusion.34
  432.5 58.2 %all-gather.4.cloned.1.call-done = bf16[256,2048]{1,0:T(8,128)(2,1)} async-done(((bf16[256,256]{1,0:T(8,128)(2,1)}), bf16[256,2048]{1,0:T(8,128)(2,1)}) %all-gather.4.cloned.1.call-update) | async-done | bytes 1048592 | tf_op jit(solution)/shard_map/all_gather | solution.py:108
  490.6 1.7 fusion.30
  492.3 2.3 fusion.114
  494.7 0.7 fusion.118
  495.5 0.5 convolution_bitcast_fusion
  496.0 0.5 convolution_bitcast_fusion.1
  496.5 0.2 fusion.99
  496.7 8.1 fusion.61
  504.9 14.5 %bitcast_reduce_fusion = (f32[256,4]{0,1:T(4,128)S(1)}, f32[256,4]{0,1:T(4,128)S(1)}, f32[4096,256,4]{1,0,2:T(8,128)}) fusion(pred[4096]{0:T(1024)(128)(4,1)S(1)} %pad_add_fusion, f32[4096,256,4]{1,0,2:T(8,128)} %fusion.61, bf16[256,4,32]{0,2,1:T(8,128)(2,1)S(1)} %get-tuple-element.13, bf16[256,4,32]{0,2,1:T(8,128)(2,1)S(1)} %get-tuple-element.12, ...), kind=kOutput, calls=%fused_computation.1 | convolution fusion | flops 564393984 | bytes 34222080 | tf_op jit(solution)/shard_map/bcgd,kcd->bcgk/dot_general | solution.py:35
  519.4 14.2 %fusion.8 = (f32[256,4]{0,1:T(4,128)S(1)}, f32[256,4]{0,1:T(4,128)S(1)}) fusion(f32[4096,256,4]{1,0,2:T(8,128)} %get-tuple-element.26, f32[256,4]{0,1:T(4,128)S(1)} %get-tuple-element.4, pred[4096]{0:T(1024)(128)(4,1)S(1)} %pad_add_fusion, f32[256,4]{0,1:T(4,128)S(1)} %get-tuple-element.5, f32[4096,256,4]{1,0,2:T(8,128)} %fusion.61), kind=kLoop, calls=%fused_computation.16 | loop fusion | flops 41940992 | bytes 33574912 | tf_op jit(solution)/shard_map/reduce_sum | solution.py:39
  533.6 0.5 fusion.46
  534.2 5.4 fusion.51
  539.7 1.5 convolution_convert_fusion.3
  541.1 0.5 fusion.47
  541.7 5.1 fusion.57
  546.8 1.4 convolution_convert_fusion.1
  548.3 0.3 reduce-scatter.7.cloned.1.call-start
  548.6 190.4 %all-reduce.3.cloned.1.call-done = (bf16[256,2048]{1,0:T(8,128)(2,1)}, bf16[256,2048]{1,0:T(8,128)(2,1)}) async-done(((bf16[256,2048]{1,0:T(8,128)(2,1)}, bf16[256,2048]{1,0:T(8,128)(2,1)}), (bf16[256,2048]{1,0:T(8,128)(2,1)}, bf16[256,2048]{1,0:T(8,128)(2,1)})) %all-reduce.3.cloned.1.call-update) | async-done | bytes 2097168 | tf_op jit(solution)/shard_map/psum | solution.py:136
  739.0 2.2 fusion.24
  741.2 1.0 copy-done.4
  742.2 1.9 fusion.78
  744.2 6.6 convolution_convert_fusion.2
  750.9 2.2 fusion.27
  753.1 0.9 copy-done.5
  754.1 1.9 fusion.74
  756.0 6.6 convolution_convert_fusion
  762.7 72.8 %reduce-scatter.7.cloned.1.call-done = bf16[256,256]{1,0:T(8,128)(2,1)} async-done(((bf16[256,2048]{1,0:T(8,128)(2,1)}), bf16[256,256]{1,0:T(8,128)(2,1)}) %reduce-scatter.7.cloned.1.call-update) | async-done | bytes 131088 | tf_op jit(solution)/shard_map/reduce_scatter | solution.py:144
  835.4 1.7 add_convert_fusion.1
  837.1 85.7 %reduce-scatter.11.cloned.1.call-done = bf16[256,256]{1,0:T(8,128)(2,1)} async-done(((bf16[256,2048]{1,0:T(8,128)(2,1)}), bf16[256,256]{1,0:T(8,128)(2,1)}) %reduce-scatter.11.cloned.1.call-update) | async-done | bytes 131088 | tf_op jit(solution)/shard_map/reduce_scatter | solution.py:144
  922.8 1.7 add_convert_fusion
  (79 shorter events, 0.6 us)
Async XLA Ops:
  7.2 737.0 %copy-start = (bf16[704,2048]{1,0:T(8,128)(2,1)S(1)}, bf16[704,2048]{1,0:T(8,128)(2,1)}, u32[]{:S(2)}) copy-start(bf16[704,2048]{1,0:T(8,128)(2,1)} %param.31) | copy-start | bytes 8650756
  8.6 46.0 %all-to-all-start = ((s32[32,1,256]{2,1,0:T(1,128)}), s32[32,1,256]{2,1,0:T(1,128)S(1)}, u32[]{:S(2)}, u32[]{:S(2)}) async-start(s32[32,1,256]{2,1,0:T(1,128)} %stack.2), calls=%async_computation | async-start | bytes 65536 | tf_op jit(solution)/shard_map/all_to_all | solution.py:91
  17.8 180.7 %reduce-scatter.9.cloned.1.call-start = ((), (), s32[]{:S(2)}) async-start(), calls=%async_computation.8 | async-start | bytes 4325376 | tf_op jit(solution)/shard_map/reduce_scatter | solution.py:98
  61.0 0.9 copy-start.11
  61.0 289.8 %reduce-scatter.5.cloned.1.call-start = ((), (), s32[]{:S(2)}) async-start(), calls=%async_computation.5 | async-start | bytes 4325376 | tf_op jit(solution)/shard_map/reduce_scatter | solution.py:95
  67.4 283.6 %copy-start.6 = (bf16[2048,64]{0,1:T(8,128)(2,1)S(1)}, bf16[2048,64]{0,1:T(8,128)(2,1)}, u32[]{:S(2)}) copy-start(bf16[2048,64]{0,1:T(8,128)(2,1)} %param.32) | copy-start | bytes 786436
  67.4 286.4 %copy-start.16 = (s32[32]{0:T(128)S(1)}, s32[32]{0:T(128)}, u32[]{:S(2)}) copy-start(s32[32]{0:T(128)} %param.20) | copy-start | bytes 388
  67.4 287.0 %copy-start.17 = (s32[32]{0:T(128)S(1)}, s32[32]{0:T(128)}, u32[]{:S(2)}) copy-start(s32[32]{0:T(128)} %param.21) | copy-start | bytes 388
  67.4 424.9 %copy-start.14 = (f32[2048]{0:T(1024)S(1)}, f32[2048]{0:T(1024)}, u32[]{:S(2)}) copy-start(f32[2048]{0:T(1024)} %param.23) | copy-start | bytes 24580
  67.4 363.5 %all-gather.6.cloned.1.call-start = ((), (), s32[]{:S(2)}) async-start(), calls=%async_computation.9 | async-start | bytes 1179648 | tf_op jit(solution)/shard_map/all_gather | solution.py:108
  198.5 292.1 %all-gather.4.cloned.1.call-start = ((), (), s32[]{:S(2)}) async-start(), calls=%async_computation.6 | async-start | bytes 1179648 | tf_op jit(solution)/shard_map/all_gather | solution.py:108
  350.9 388.1 %all-reduce.3.cloned.1.call-start = ((), (), s32[]{:S(2)}) async-start(), calls=%async_computation.11 | async-start | bytes 4194304 | tf_op jit(solution)/shard_map/psum | solution.py:136
  351.6 145.1 %collective-permute-start.1 = (bf16[1792,64]{0,1:T(8,128)(2,1)}, bf16[1792,64]{0,1:T(8,128)(2,1)S(1)}, u32[]{:S(2)}, u32[]{:S(2)}) collective-permute-start(bf16[1792,64]{0,1:T(8,128)(2,1)} %slice.35), channel_id=1, source_target_pairs={{0,8},{8,0},{16,24},{24,16},{32,40},{40,32},{48,56},{56,48},{64,72... | collective-permute-start | bytes 688136 | tf_op jit(solution)/shard_map/ppermute | solution.py:12
  353.3 180.8 %collective-permute-start = (bf16[1792,64]{0,1:T(8,128)(2,1)}, bf16[1792,64]{0,1:T(8,128)(2,1)}, u32[]{:S(2)}, u32[]{:S(2)}) collective-permute-start(bf16[1792,64]{0,1:T(8,128)(2,1)} %slice.33), channel_id=1, source_target_pairs={{0,8},{8,0},{16,24},{24,16},{32,40},{40,32},{48,56},{56,48},{64,72... | collective-permute-start | bytes 688136 | tf_op jit(solution)/shard_map/ppermute | solution.py:12
  490.6 4.0 copy-start.3
  490.6 4.0 copy-start.10
  492.3 3.1 copy-start.2
  492.3 3.1 copy-start.12
  504.9 29.3 %slice-start = ((s8[16777216]{0:T(1024)(128)(4,1)}), s8[4194304]{0:T(1024)(128)(4,1)S(1)}, s32[]{:S(2)}) async-start(s8[16777216]{0:T(1024)(128)(4,1)} %bitcast.173), calls=%async_computation.12 | async-start | bytes 8388608
  504.9 29.3 %slice-start.1 = ((s8[16777216]{0:T(1024)(128)(4,1)}), s8[4194304]{0:T(1024)(128)(4,1)S(1)}, s32[]{:S(2)}) async-start(s8[16777216]{0:T(1024)(128)(4,1)} %bitcast.173), calls=%async_computation.13 | async-start | bytes 8388608
  504.9 29.3 %slice-start.2 = ((s8[16777216]{0:T(1024)(128)(4,1)}), s8[4194304]{0:T(1024)(128)(4,1)S(1)}, s32[]{:S(2)}) async-start(s8[16777216]{0:T(1024)(128)(4,1)} %bitcast.173), calls=%async_computation.14 | async-start | bytes 8388608
  519.4 14.2 %copy-start.13 = (bf16[2048,64]{0,1:T(8,128)(2,1)S(1)}, bf16[2048,64]{0,1:T(8,128)(2,1)}, u32[]{:S(2)}) copy-start(bf16[2048,64]{0,1:T(8,128)(2,1)} %param.26) | copy-start | bytes 786436
  519.4 14.8 %slice-start.3 = ((s8[16777216]{0:T(1024)(128)(4,1)}), s8[4194304]{0:T(1024)(128)(4,1)S(1)}, s32[]{:S(2)}) async-start(s8[16777216]{0:T(1024)(128)(4,1)} %bitcast.173), calls=%async_computation.15 | async-start | bytes 8388608
  519.4 14.8 %copy-start.7 = (bf16[2048,64]{0,1:T(8,128)(2,1)S(1)}, bf16[2048,64]{0,1:T(8,128)(2,1)}, u32[]{:S(2)}) copy-start(bf16[2048,64]{0,1:T(8,128)(2,1)} %param.33) | copy-start | bytes 786436
  533.6 8.1 slice-start.4
  534.2 5.5 copy-start.1
  534.2 7.5 slice-start.5
  534.2 7.5 slice-start.6
  534.2 7.5 slice-start.7
  548.3 193.9 %copy-start.15 = (f32[2048]{0:T(1024)S(1)}, f32[2048]{0:T(1024)}, u32[]{:S(2)}) copy-start(f32[2048]{0:T(1024)} %param.28) | copy-start | bytes 24580
  548.3 287.1 %reduce-scatter.7.cloned.1.call-start = ((), (), s32[]{:S(2)}) async-start(), calls=%async_computation.7 | async-start | bytes 1179648 | tf_op jit(solution)/shard_map/reduce_scatter | solution.py:144
  739.0 3.2 copy-start.8
  741.2 1.0 copy-start.4
  750.8 171.9 %reduce-scatter.11.cloned.1.call-start = ((), (), s32[]{:S(2)}) async-start(), calls=%async_computation.10 | async-start | bytes 1179648 | tf_op jit(solution)/shard_map/reduce_scatter | solution.py:144
  750.9 3.2 copy-start.9
  753.1 1.0 copy-start.5
Sparse Core Ops, SparseCore 0:
  61.1 137.3 reduce-scatter.8
  201.0 149.7 reduce-scatter.4
  353.3 77.5 all-gather.5
  433.3 57.3 all-gather.3
  548.4 190.5 all-reduce.2
  750.9 84.4 reduce-scatter.6
  839.9 82.8 reduce-scatter.10
